TPU v7x, 512 devices: a whole 4x4x16 slice. The times are simulated.
512 devices in a mesh: section: 8 (over x, y_hi), vocab: 64 (over z, y_lo, core).
Axes of the slice: x: 4, y: 4 (y_hi: 2, y_lo: 2; y = y_hi * 2 + y_lo), z: 16, core: 2. Of those that a mesh axis runs over, the one named last changes fastest.
Arguments:
- hidden: bfloat16 [512, 8192], P('vocab', 'section'), may hold values from -6 to 6
- head_weight: bfloat16 [98304, 8192], P('vocab', 'section'), may hold values from -3 to 3
- lengths: int32 [8], replicated, may hold values from 16 to 64
- pairing: int32 [4], replicated, may hold values from 0 to 3, each once
Outputs:
- hidden_grad: float32 [512, 8192], P('vocab', 'section')
- loss: float32 [], replicated
Inputs may be any that keep to these rules, and one draw needn't show every extreme that they name: Every sequence has at least one live token; positions from lengths on are padding. `pairing`: a permutation: each document matches exactly one query.
All inputs are finite; a program needn't handle non-finite values.
Results may differ from a plain program's by a relative error of at most 0.0018.
Values may be sent and summed in bfloat16 or wider, within the bound.
No kernel may reach another device: no remote copies, remote signals or barrier semaphores. Data moves between devices by JAX's collectives and lax.ppermute only.
A program may use at most 64 MiB of HBM per device.

v0:
```python
import jax
import jax.numpy as jnp
from jax import lax
from jax.sharding import PartitionSpec as P

NSEQ = 8
pool_temp = 0.5
score_temp = 0.02
grad_scale = 16.0
eps_norm = 1e-06


def local(hidden, head_weight, lengths, pairing):
    half = NSEQ // 2
    partial_logits = lax.dot_general(
        lax.all_gather(hidden, "vocab", axis=0, tiled=True),
        head_weight,
        (((1,), (1,)), ((), ())),
        preferred_element_type=jnp.float32,
    )
    total_rows = partial_logits.shape[0]
    seq_len = total_rows // NSEQ
    logits = lax.psum(partial_logits, "section")
    columns = logits.shape[1]
    soft = jax.nn.softplus(logits)
    act = jnp.log1p(soft)
    positions = jnp.arange(seq_len, dtype=jnp.int32)
    live = (positions[None, :] < lengths[:, None]).astype(jnp.float32)
    expo = jnp.exp(act / pool_temp).reshape(NSEQ, seq_len, columns) * live[:, :, None]
    totals = jnp.sum(expo, axis=1)
    pooled = pool_temp * jnp.log(totals)
    queries = pooled[:half]
    documents = pooled[half:]
    dots_part = lax.dot_general(
        queries, documents, (((1,), (1,)), ((), ())), precision=lax.Precision.HIGHEST
    )
    norms_part = jnp.sum(pooled * pooled, axis=1)
    dots, norms = lax.psum((dots_part, norms_part), "vocab")
    inv = lax.rsqrt(norms + eps_norm)
    inv_q = inv[:half]
    inv_d = inv[half:]
    scores = dots * inv_q[:, None] * inv_d[None, :] / score_temp
    weights = jnp.exp(scores)
    row_sum = jnp.sum(weights, axis=1)
    probs = weights / row_sum[:, None]
    target = (jnp.arange(half, dtype=jnp.int32)[None, :] == pairing[:, None]).astype(jnp.float32)
    loss = jnp.sum(jnp.log(row_sum) - jnp.sum(scores * target, axis=1))
    dscore = grad_scale * (probs - target)
    gdots = dscore * inv_q[:, None] * inv_d[None, :] / score_temp
    dinv_q = jnp.sum(dscore * dots * inv_d[None, :], axis=1) / score_temp
    dinv_d = jnp.sum(dscore * dots * inv_q[:, None], axis=0) / score_temp
    dinv = jnp.concatenate([dinv_q, dinv_d])
    dnorm = -0.5 * dinv * inv * inv * inv
    dpool_q = (
        jnp.dot(gdots, documents, precision=lax.Precision.HIGHEST)
        + 2.0 * dnorm[:half, None] * queries
    )
    dpool_d = (
        jnp.dot(gdots.T, queries, precision=lax.Precision.HIGHEST)
        + 2.0 * dnorm[half:, None] * documents
    )
    dpooled = jnp.concatenate([dpool_q, dpool_d], axis=0)
    dact = (dpooled[:, None, :] * expo / totals[:, None, :]).reshape(total_rows, columns)
    dlogit = (dact * jax.nn.sigmoid(logits) / (1.0 + soft)).astype(jnp.bfloat16)
    hidden_grad = lax.psum_scatter(
        jnp.dot(dlogit, head_weight, preferred_element_type=jnp.float32),
        "vocab",
        scatter_dimension=0,
        tiled=True,
    )
    return (hidden_grad, loss)


def solution(mesh):
    in_specs = (P("vocab", "section"), P("vocab", "section"), P(), P())
    out_specs = (P("vocab", "section"), P())
    return jax.shard_map(local, mesh=mesh, in_specs=in_specs, out_specs=out_specs, check_vma=False)
```

profile of v0, /device:TPU:2, one launch (start us, length us, event | category | flops | bytes accessed | tf_op | source)
XLA Modules:
  0.0 654.5 jit_solution(2297248620862196060)
XLA Ops:
  7.2 0.0 copy-start
  7.2 0.0 all-gather.2.cloned.1.call-start
  7.2 0.7 all-gather.2.cloned.1.call-update
  7.9 0.0 all-reduce.3.cloned.1.call-start
  8.0 127.2 %all-gather.2.cloned.1.call-done = bf16[512,1024]{1,0:T(8,128)(2,1)} async-done(((bf16[8,1024]{1,0:T(8,128)(2,1)}), bf16[512,1024]{1,0:T(8,128)(2,1)}) %all-gather.2.cloned.1.call-update) | async-done | bytes 1048592 | tf_op jit(solution)/shard_map/all_gather | solution.py:16
  135.2 0.0 copy-done
  135.2 4.7 fusion.17
  139.9 0.0 copy-start.1
  139.9 0.0 all-reduce.3.cloned.1.call-update
  140.0 0.0 copy-start.2
  140.0 0.0 reduce-scatter.2.cloned.1.call-start
  140.0 0.6 copy-done.1
  140.6 0.1 fusion.8
  140.7 0.1 reshape.50
  140.7 157.0 %all-reduce.3.cloned.1.call-done = f32[512,1536]{1,0:T(8,128)} async-done(((f32[512,1536]{1,0:T(8,128)}), f32[512,1536]{1,0:T(8,128)}) %all-reduce.3.cloned.1.call-update) | async-done | bytes 3145744 | tf_op jit(solution)/shard_map/psum | solution.py:23
  297.7 5.1 multiply_reduce_fusion
  302.8 0.1 multiply_reduce_fusion.1
  302.9 0.2 fusion.4
  303.1 108.1 %all-reduce = (f32[8]{0:T(128)S(1)}, f32[4,4]{1,0:T(4,128)S(1)}) all-reduce(f32[8]{0:T(128)S(1)} %get-tuple-element.8, f32[4,4]{1,0:T(4,128)S(1)} %fusion.4), channel_id=1, replica_groups=mesh['section'=8,'vocab'=64] {'vocab'}, use_global_device_ids=true, to_apply=%region_4.5 | all-reduce | flops 24 | bytes 192 | tf_op jit(solution)/shard_map/psum | solution.py:38
  411.2 0.1 broadcast_multiply_fusion.2
  411.3 0.2 exponential_reduce_fusion
  411.4 0.0 copy-done.2
  411.5 0.2 multiply_reduce_fusion.3
  411.7 0.1 multiply_multiply_fusion.5
  411.7 0.1 slice_multiply_fusion.1
  411.8 0.2 convolution_add_fusion.1
  412.1 0.3 convolution_add_fusion
  412.4 5.5 fusion.2
  418.0 3.2 fusion.18
  421.2 0.0 reduce-scatter.2.cloned.1.call-update
  421.2 0.6 subtract_reduce_fusion
  421.8 226.2 %reduce-scatter.2.cloned.1.call-done = f32[8,1024]{1,0:T(8,128)} async-done(((f32[512,1024]{1,0:T(8,128)}), f32[8,1024]{1,0:T(8,128)}) %reduce-scatter.2.cloned.1.call-update) | async-done | bytes 32784 | tf_op jit(solution)/shard_map/reduce_scatter | solution.py:65
  (3 shorter events, 0.0 us)
Async XLA Ops:
  7.2 128.0 %copy-start = (bf16[1536,1024]{1,0:T(8,128)(2,1)S(1)}, bf16[1536,1024]{1,0:T(8,128)(2,1)}, u32[]{:S(2)}) copy-start(bf16[1536,1024]{1,0:T(8,128)(2,1)} %param.5) | copy-start | bytes 9437188
  7.2 128.0 %all-gather.2.cloned.1.call-start = ((), (), s32[]{:S(2)}) async-start(), calls=%async_computation.1 | async-start | bytes 1064960 | tf_op jit(solution)/shard_map/all_gather | solution.py:16
  7.9 289.8 %all-reduce.3.cloned.1.call-start = ((), (), s32[]{:S(2)}) async-start(), calls=%async_computation.2 | async-start | bytes 6291456 | tf_op jit(solution)/shard_map/psum | solution.py:23
  139.9 0.7 copy-start.1
  140.0 271.5 %copy-start.2 = (s32[4]{0:T(128)S(1)}, s32[4]{0:T(128)}, u32[]{:S(2)}) copy-start(s32[4]{0:T(128)} %param.7) | copy-start | bytes 52
  140.0 508.0 %reduce-scatter.2.cloned.1.call-start = ((), (), s32[]{:S(2)}) async-start(), calls=%async_computation.3 | async-start | bytes 2129920 | tf_op jit(solution)/shard_map/reduce_scatter | solution.py:65
Sparse Core Ops, SparseCore 0:
  10.2 124.9 all-gather.1
  140.1 157.6 all-reduce.2
  421.3 226.6 reduce-scatter.1
where the time goes:
time: 655 us
  waiting for transfers between devices  511 us (78%)
  blocking collectives  108 us (16%)
  between operations  13.8 us (2%)
  other arithmetic  12 us (2%)
  matrix products  8.66 us (1%)
    reduce_scatter x1, waiting for transfers between devices, local(): lax.psum_scatter(jnp.dot(dlogit, head_weight, preferred_element_type=jnp....  226 us
    psum x1, waiting for transfers between devices, local(): logits = lax.psum(partial_logits, 'section')  157 us
    all_gather x1, waiting for transfers between devices, local(): lax.all_gather(hidden, 'vocab', axis=0, tiled=True)  127 us
    psum x1, blocking collectives, local(): dots, norms = lax.psum((dots_part, norms_part), 'vocab')  108 us
  transfers between devices with their start and end apart: 3, of which 3 were waited for; matrix products, arithmetic and copies ran while one was open for 0% of the time, Pallas kernels for 0%

commit v1 on v0

--- a/solution.py
+++ b/solution.py
@@ -10,6 +10,12 @@
 eps_norm = 1e-06
 
 
+def add_all(x, mesh_axis):
+    parts = lax.all_gather(x, mesh_axis, axis=0, tiled=False)
+    summed = parts.sum(axis=0)
+    return summed
+
+
 def local(hidden, head_weight, lengths, pairing):
     half = NSEQ // 2
     partial_logits = lax.dot_general(
@@ -20,7 +26,7 @@
     )
     total_rows = partial_logits.shape[0]
     seq_len = total_rows // NSEQ
-    logits = lax.psum(partial_logits, "section")
+    logits = add_all(partial_logits, "section")
     columns = logits.shape[1]
     soft = jax.nn.softplus(logits)
     act = jnp.log1p(soft)

time: 655 us -> 781 us (1.19)
  waiting for transfers between devices: 511 us -> 625 us
  other arithmetic: 12 us -> 24 us
    all_gather x0 -> x1, waiting for transfers between devices: none -> 273 us  [add_all(): parts = lax.all_gather(x, mesh_axis, axis=0, tiled=False)]
    psum x1 -> x0, waiting for transfers between devices: 157 us -> none  [local(): logits = lax.psum(partial_logits, 'section')]
    reduce_sum x0 -> x1, other arithmetic: none -> 11.9 us  [add_all(): summed = parts.sum(axis=0)]
where the time goes in v1:
time: 781 us; the launch traced here: 780 us
  waiting for transfers between devices  625 us (80%)
  blocking collectives  108 us (14%)
  other arithmetic  24 us (3%)
  between operations  13.8 us (2%)
  matrix products  8.75 us (1%)
    all_gather x1, waiting for transfers between devices, add_all(): parts = lax.all_gather(x, mesh_axis, axis=0, tiled=False)  273 us
    reduce_scatter x1, waiting for transfers between devices, local(): lax.psum_scatter(jnp.dot(dlogit, head_weight, preferred_element_type=jnp....  224 us
    all_gather x1, waiting for transfers between devices, local(): lax.all_gather(hidden, 'vocab', axis=0, tiled=True)  127 us
    psum x1, blocking collectives, local(): dots, norms = lax.psum((dots_part, norms_part), 'vocab')  108 us
  transfers between devices with their start and end apart: 3, of which 3 were waited for; matrix products, arithmetic and copies ran while one was open for 0% of the time, Pallas kernels for 0%

profile of v1, /device:TPU:2, one launch (start us, length us, event | category | flops | bytes accessed | tf_op | source)
XLA Modules:
  0.0 780.5 jit_solution(6300930750134485920)
XLA Ops:
  7.2 0.0 copy-start
  7.2 0.0 all-gather.4.cloned.1.call-start
  7.2 0.7 all-gather.4.cloned.1.call-update
  7.9 0.0 all-gather.6.cloned.1.call-start
  8.0 127.2 %all-gather.4.cloned.1.call-done = bf16[512,1024]{1,0:T(8,128)(2,1)} async-done(((bf16[8,1024]{1,0:T(8,128)(2,1)}), bf16[512,1024]{1,0:T(8,128)(2,1)}) %all-gather.4.cloned.1.call-update) | async-done | bytes 1048592 | tf_op jit(solution)/shard_map/all_gather | solution.py:22
  135.2 0.0 copy-done
  135.2 4.8 fusion.22
  140.0 0.0 copy-start.1
  140.0 0.0 all-gather.6.cloned.1.call-update
  140.0 0.0 reduce-scatter.2.cloned.1.call-start
  140.1 0.6 copy-done.1
  140.7 0.1 fusion.13
  140.7 0.1 reshape.48
  140.8 273.0 %all-gather.6.cloned.1.call-done = f32[4096,1536]{1,0:T(8,128)} async-done(((f32[512,1536]{1,0:T(8,128)}), f32[4096,1536]{1,0:T(8,128)}) %all-gather.6.cloned.1.call-update) | async-done | bytes 25165840 | tf_op jit(solution)/shard_map/all_gather | solution.py:14
  413.8 11.9 %reduce_sum.74 = f32[512,1536]{1,0:T(8,128)} reduce(f32[8,512,1536]{2,1,0:T(8,128)} %bitcast.24, f32[]{:T(128)} %constant.8.clone.1), dimensions={0}, to_apply=%region_0.0 | reduce | flops 5505024 | bytes 28311556 | tf_op jit(solution)/shard_map/reduce_sum | solution.py:15
  425.8 0.0 copy-start.2
  425.8 5.1 fusion.4
  430.8 0.1 multiply_reduce_fusion
  431.0 0.2 fusion.9
  431.1 107.8 %all-reduce = (f32[8]{0:T(128)S(1)}, f32[4,4]{1,0:T(4,128)S(1)}) all-reduce(f32[8]{0:T(128)S(1)} %get-tuple-element.8, f32[4,4]{1,0:T(4,128)S(1)} %fusion.9), channel_id=1, replica_groups=mesh['section'=8,'vocab'=64] {'vocab'}, use_global_device_ids=true, to_apply=%region_4.5 | all-reduce | flops 24 | bytes 192 | tf_op jit(solution)/shard_map/psum | solution.py:44
  538.9 0.1 broadcast_multiply_fusion.2
  539.0 0.2 exponential_reduce_fusion
  539.2 0.0 copy-done.2
  539.2 0.2 multiply_reduce_fusion.2
  539.4 0.1 multiply_multiply_fusion.5
  539.5 0.1 slice_multiply_fusion.1
  539.6 0.3 convolution_add_fusion.1
  539.8 0.3 convolution_add_fusion
  540.2 5.5 fusion.7
  545.7 3.2 fusion.23
  548.9 0.0 reduce-scatter.2.cloned.1.call-update
  548.9 0.6 subtract_reduce_fusion
  549.6 224.4 %reduce-scatter.2.cloned.1.call-done = f32[8,1024]{1,0:T(8,128)} async-done(((f32[512,1024]{1,0:T(8,128)}), f32[8,1024]{1,0:T(8,128)}) %reduce-scatter.2.cloned.1.call-update) | async-done | bytes 32784 | tf_op jit(solution)/shard_map/reduce_scatter | solution.py:71
  (3 shorter events, 0.0 us)
Async XLA Ops:
  7.2 128.0 %copy-start = (bf16[1536,1024]{1,0:T(8,128)(2,1)S(1)}, bf16[1536,1024]{1,0:T(8,128)(2,1)}, u32[]{:S(2)}) copy-start(bf16[1536,1024]{1,0:T(8,128)(2,1)} %param.5) | copy-start | bytes 9437188
  7.2 128.0 %all-gather.4.cloned.1.call-start = ((), (), s32[]{:S(2)}) async-start(), calls=%async_computation.1 | async-start | bytes 1064960 | tf_op jit(solution)/shard_map/all_gather | solution.py:22
  7.9 405.9 %all-gather.6.cloned.1.call-start = ((), (), s32[]{:S(2)}) async-start(), calls=%async_computation.3 | async-start | bytes 28311552 | tf_op jit(solution)/shard_map/all_gather | solution.py:14
  140.0 0.7 copy-start.1
  140.0 633.9 %reduce-scatter.2.cloned.1.call-start = ((), (), s32[]{:S(2)}) async-start(), calls=%async_computation.2 | async-start | bytes 2129920 | tf_op jit(solution)/shard_map/reduce_scatter | solution.py:71
  425.8 113.4 %copy-start.2 = (s32[4]{0:T(128)S(1)}, s32[4]{0:T(128)}, u32[]{:S(2)}) copy-start(s32[4]{0:T(128)} %param.7) | copy-start | bytes 52
Sparse Core Ops, SparseCore 0:
  10.2 124.9 all-gather.3
  140.2 273.6 all-gather.5
  549.1 224.8 reduce-scatter.1

commit v2 on v0

--- a/solution.py
+++ b/solution.py
@@ -2,6 +2,7 @@
 import jax.numpy as jnp
 from jax import lax
 from jax.sharding import PartitionSpec as P
+from jax.lax import all_to_all, axis_size
 
 NSEQ = 8
 pool_temp = 0.5
@@ -11,9 +12,20 @@
 
 
 def local(hidden, head_weight, lengths, pairing):
+
+    def _guide_boxes(work_x, group_axis):
+        x_new = all_to_all(
+            jnp.stack([work_x] * axis_size(group_axis), axis=0),
+            concat_axis=0,
+            axis_name=group_axis,
+            split_axis=0,
+        )
+        all_rows = jnp.concatenate(x_new, 0)
+        return all_rows
+
     half = NSEQ // 2
     partial_logits = lax.dot_general(
-        lax.all_gather(hidden, "vocab", axis=0, tiled=True),
+        _guide_boxes(hidden, "vocab"),
         head_weight,
         (((1,), (1,)), ((), ())),
         preferred_element_type=jnp.float32,

time: 655 us -> 596 us (0.910)
  waiting for transfers between devices: 511 us -> 379 us
  blocking collectives: 108 us -> 181 us
    all_gather x1 -> x0, waiting for transfers between devices: 127 us -> none  [local(): lax.all_gather(hidden, 'vocab', axis=0, tiled=True)]
    all_to_all x0 -> x1, blocking collectives: none -> 73.1 us  [_guide_boxes(): all_to_all(jnp.stack([work_x] * axis_size(group_axis), axis=0), concat_ax...]
  transfers between devices with their start and end apart: 3 -> 2, of which waited for: 3 -> 2; matrix products, arithmetic and copies ran while one was open for 0% -> 0% of each run, Pallas kernels for 0% -> 0%
where the time goes in v2:
time: 596 us
  waiting for transfers between devices  379 us (64%)
  blocking collectives  181 us (30%)
  between operations  14.1 us (2%)
  other arithmetic  12 us (2%)
  matrix products  7.5 us (1%)
    reduce_scatter x1, waiting for transfers between devices, local(): lax.psum_scatter(jnp.dot(dlogit, head_weight, preferred_element_type=jnp....  226 us
    psum x1, waiting for transfers between devices, local(): logits = lax.psum(partial_logits, 'section')  153 us
    psum x1, blocking collectives, local(): dots, norms = lax.psum((dots_part, norms_part), 'vocab')  108 us
    all_to_all x1, blocking collectives, _guide_boxes(): all_to_all(jnp.stack([work_x] * axis_size(group_axis), axis=0), concat_ax...  73.1 us
  transfers between devices with their start and end apart: 2, of which 2 were waited for; matrix products, arithmetic and copies ran while one was open for 0% of the time, Pallas kernels for 0%

profile of v2, /device:TPU:2, one launch (start us, length us, event | category | flops | bytes accessed | tf_op | source)
XLA Modules:
  0.0 595.6 jit_solution(6950216735271630731)
XLA Ops:
  7.2 0.0 copy-start
  7.2 0.0 all-reduce.3.cloned.1.call-start
  7.2 1.0 stack.2
  8.2 73.1 %all_to_all.5 = bf16[64,8,1024]{2,1,0:T(8,128)(2,1)S(1)} all-to-all(bf16[64,8,1024]{2,1,0:T(8,128)(2,1)S(1)} %stack.2), channel_id=1, replica_groups=mesh['section'=8,'vocab'=64] {'vocab'}, dimensions={0} | all-to-all | bytes 2097152 | tf_op jit(solution)/shard_map/all_to_all | solution.py:17
  81.3 0.0 copy-done
  81.3 3.6 fusion.3
  84.8 0.0 copy-start.1
  84.8 0.0 all-reduce.3.cloned.1.call-update
  84.9 0.0 copy-start.2
  84.9 0.0 reduce-scatter.2.cloned.1.call-start
  84.9 0.6 copy-done.1
  85.5 0.1 fusion.10
  85.6 0.1 reshape.56
  85.6 152.9 %all-reduce.3.cloned.1.call-done = f32[512,1536]{1,0:T(8,128)} async-done(((f32[512,1536]{1,0:T(8,128)}), f32[512,1536]{1,0:T(8,128)}) %all-reduce.3.cloned.1.call-update) | async-done | bytes 3145744 | tf_op jit(solution)/shard_map/psum | solution.py:35
  238.5 5.1 multiply_reduce_fusion
  243.6 0.1 multiply_reduce_fusion.1
  243.7 0.2 fusion.6
  243.9 108.1 %all-reduce = (f32[8]{0:T(128)S(1)}, f32[4,4]{1,0:T(4,128)S(1)}) all-reduce(f32[8]{0:T(128)S(1)} %get-tuple-element.8, f32[4,4]{1,0:T(4,128)S(1)} %fusion.6), channel_id=1, replica_groups=mesh['section'=8,'vocab'=64] {'vocab'}, use_global_device_ids=true, to_apply=%region_4.5 | all-reduce | flops 24 | bytes 192 | tf_op jit(solution)/shard_map/psum | solution.py:50
  351.9 0.1 broadcast_multiply_fusion.2
  352.0 0.2 exponential_reduce_fusion
  352.2 0.0 copy-done.2
  352.2 0.2 multiply_reduce_fusion.3
  352.4 0.1 multiply_multiply_fusion.5
  352.5 0.1 slice_multiply_fusion.1
  352.6 0.2 convolution_add_fusion.1
  352.8 0.3 convolution_add_fusion
  353.2 5.5 fusion.2
  358.7 3.2 fusion.19
  361.9 0.0 reduce-scatter.2.cloned.1.call-update
  362.0 0.6 subtract_reduce_fusion
  362.6 226.2 %reduce-scatter.2.cloned.1.call-done = f32[8,1024]{1,0:T(8,128)} async-done(((f32[512,1024]{1,0:T(8,128)}), f32[8,1024]{1,0:T(8,128)}) %reduce-scatter.2.cloned.1.call-update) | async-done | bytes 32784 | tf_op jit(solution)/shard_map/reduce_scatter | solution.py:77
  (3 shorter events, 0.0 us)
Async XLA Ops:
  7.2 74.1 %copy-start = (bf16[1536,1024]{1,0:T(8,128)(2,1)S(1)}, bf16[1536,1024]{1,0:T(8,128)(2,1)}, u32[]{:S(2)}) copy-start(bf16[1536,1024]{1,0:T(8,128)(2,1)} %param.5) | copy-start | bytes 9437188
  7.2 231.3 %all-reduce.3.cloned.1.call-start = ((), (), s32[]{:S(2)}) async-start(), calls=%async_computation.2 | async-start | bytes 6291456 | tf_op jit(solution)/shard_map/psum | solution.py:35
  84.8 0.7 copy-start.1
  84.9 267.4 %copy-start.2 = (s32[4]{0:T(128)S(1)}, s32[4]{0:T(128)}, u32[]{:S(2)}) copy-start(s32[4]{0:T(128)} %param.7) | copy-start | bytes 52
  84.9 503.9 %reduce-scatter.2.cloned.1.call-start = ((), (), s32[]{:S(2)}) async-start(), calls=%async_computation.3 | async-start | bytes 2129920 | tf_op jit(solution)/shard_map/reduce_scatter | solution.py:77
Sparse Core Ops, SparseCore 0:
  85.0 153.4 all-reduce.2
  362.1 226.6 reduce-scatter.1
